TPU v7x, 32 devices: a whole 2x2x4 slice. The times are simulated.
32 devices in a mesh: clips: 2 (over y), frame: 4 (over x, core), row: 4 (over z).
Axes of the slice: x: 2, y: 2, z: 4, core: 2. Of those that a mesh axis runs over, the one named last changes fastest.
Arguments:
- frames: bfloat16 [16, 512, 640], P(('clips', 'frame'), 'row'), parts along dimension 0, may hold values from -16 to 16
- key_index: int32 [4], P('clips'), parts along dimension 0, may hold values from 0 to 7, as said below
- w_query: bfloat16 [640, 640], replicated, may hold values from -0.25 to 0.25
- w_keyval: bfloat16 [640, 1280], replicated, may hold values from -0.25 to 0.25
- w_out: bfloat16 [640, 640], replicated, may hold values from -0.25 to 0.25
- norm_gain: float32 [640], replicated, may hold values from 0.1 to 1.9
- w_first: bfloat16 [3, 640, 640], replicated, may hold values from -0.125 to 0.125
- w_second: bfloat16 [3, 640, 640], replicated, may hold values from -0.125 to 0.125
Outputs:
- edited: bfloat16 [16, 512, 640], P(('clips', 'frame'), 'row'), parts along dimension 0
There are 2 independent parts, one for each index of `clips`. A program takes and returns all parts, laid end to end along the dimension named above; an argument that names none is the same for every part. Nothing has to cross between parts.
Inputs may be any that keep to these rules, and one draw needn't show every extreme that they name: `key_index`: two different frame indices of the window, in either order; one of them is the window's last frame 8 - 1.
All inputs are finite; a program needn't handle non-finite values.
Results may differ from a plain program's by a relative error of at most 0.0067.
Values may be sent and summed in bfloat16 or wider, within the bound.
No kernel may reach another device: no remote copies, remote signals or barrier semaphores. Data moves between devices by JAX's collectives and lax.ppermute only.
A program may use at most 128 MiB of HBM per device.

v0:
```python
from functools import partial
import jax
import jax.numpy as jnp
from jax import lax
from jax.sharding import PartitionSpec as P

HEADS = 10
HEAD_DIM = 64


def from_root(value, axis, source):
    kept = jnp.where(lax.axis_index(axis) == source, value, 0).astype(value.dtype)
    return lax.psum(kept, axis)


def extended(array, sides, width):
    for axis, dim in sides:
        size, length = (lax.axis_size(axis), array.shape[dim])
        up = [(i, (i + 1) % size) for i in range(size - 1)]
        down = [(j, i) for i, j in up]
        last = lax.slice_in_dim(array, length - width, length, axis=dim)
        first = lax.slice_in_dim(array, 0, width, axis=dim)
        before = lax.ppermute(last, axis, up)
        after = lax.ppermute(first, axis, down)
        array = jnp.concatenate([before, array, after], axis=dim)
    return array


def temporal_mix(padded, weights, count):
    result = jnp.zeros((count * padded.shape[1], padded.shape[2]), jnp.float32)
    for offset in range(3):
        window = padded[offset : offset + count].reshape(-1, padded.shape[2])
        result = result + jnp.dot(window, weights[offset], preferred_element_type=jnp.float32)
    return result


def absorb_keys(query_heads, channels, state_now, kv_pieces, piece_start):
    highest, denominator, accumulated = state_now
    joined = jnp.concatenate(kv_pieces, axis=0)
    key_heads = joined[:, :channels].reshape(-1, HEADS, HEAD_DIM)
    value_heads = joined[:, channels:].reshape(-1, HEADS, HEAD_DIM)
    scores = jnp.einsum(
        "qhd,khd->hqk", query_heads, key_heads, preferred_element_type=jnp.float32
    ) * HEAD_DIM ** (-0.5)
    raised = jnp.maximum(highest, jnp.max(scores, axis=-1))
    kept_frac = jnp.exp(highest - raised)
    exponent = jnp.exp(scores - raised[:, :, None])
    denominator = jnp.sum(exponent, axis=-1)
    contrib = jnp.einsum(
        "hqk,khd->qhd",
        exponent.astype(jnp.bfloat16),
        value_heads,
        preferred_element_type=jnp.float32,
    )
    accumulated = accumulated * jnp.repeat(kept_frac.T, HEAD_DIM, axis=1) + contrib.reshape(
        contrib.shape[0], -1
    )
    return (raised, denominator, accumulated)


def shards(frames, key_index, w_query, w_keyval, w_out, norm_gain, w_first, w_second):
    frame_count, row_count, channels = frames.shape
    flattened = frames.reshape(-1, channels)
    queries = jnp.dot(flattened, w_query, preferred_element_type=jnp.float32).astype(jnp.bfloat16)
    query_heads = queries.reshape(-1, HEADS, HEAD_DIM)
    query_total = queries.shape[0]
    owners = key_index // frame_count
    chosen = frames[key_index % frame_count].reshape(-1, channels)
    keyval = jnp.dot(chosen, w_keyval, preferred_element_type=jnp.float32).astype(jnp.bfloat16)
    own_parts = (keyval[:row_count], keyval[row_count:])
    initial = (
        jnp.full((HEADS, query_total), -1e30, jnp.float32),
        jnp.zeros((HEADS, query_total), jnp.float32),
        jnp.zeros((query_total, channels), jnp.float32),
    )
    absorb = partial(absorb_keys, query_heads, channels)
    spread_parts = []
    for key_slot in range(2):
        spread_parts.append(from_root(own_parts[key_slot], "frame", owners[key_slot]))
    final = absorb(
        initial,
        (
            lax.all_gather(spread_parts[0], "row", axis=0, tiled=True),
            lax.all_gather(spread_parts[1], "row", axis=0, tiled=True),
        ),
        jnp.int32(0),
    )
    highest, denominator, accumulated = final
    mixed = accumulated.reshape(query_total, HEADS, HEAD_DIM) / denominator.T[:, :, None]
    attended = mixed.reshape(query_total, channels).astype(jnp.bfloat16)
    residual = flattened.astype(jnp.float32) + jnp.dot(
        attended, w_out, preferred_element_type=jnp.float32
    )
    mean_square = jnp.mean(residual * residual, axis=-1, keepdims=True)
    normed = (residual * lax.rsqrt(mean_square + 1e-06) * norm_gain).astype(jnp.bfloat16)
    normed = normed.reshape(frame_count, row_count, channels)
    padded = extended(normed, (("frame", 0),), 1)
    hidden = jax.nn.silu(temporal_mix(padded, w_first, frame_count)).astype(jnp.bfloat16)
    hidden = hidden.reshape(frame_count, row_count, channels)
    padded = extended(hidden, (("frame", 0),), 1)
    second = temporal_mix(padded, w_second, frame_count)
    return (residual + second).astype(jnp.bfloat16).reshape(frame_count, row_count, channels)


def solution(mesh):
    return jax.shard_map(
        shards,
        mesh=mesh,
        in_specs=(P(("clips", "frame"), "row", None), P("clips"), P(), P(), P(), P(), P(), P()),
        out_specs=P(("clips", "frame"), "row", None),
        check_vma=False,
    )
```

profile of v0, /device:TPU:1, one launch (start us, length us, event | category | flops | bytes accessed | tf_op | source)
XLA Modules:
  0.0 162.4 jit_solution(13678371207064377667)
XLA Ops:
  6.5 0.0 copy-start
  6.5 0.0 all-reduce.3.cloned.1.call-start
  6.5 0.8 and_select_fusion.1
  7.3 0.6 fusion.42
  9.2 1.6 gather_fusion
  10.8 0.0 copy-done
  10.8 0.0 copy-start.1
  10.8 0.0 copy-start.5
  10.8 0.7 convolution_convert_fusion
  11.5 0.9 slice_select_fusion
  12.4 0.0 all-reduce.3.cloned.1.call-update
  12.5 0.0 all-gather.3.cloned.1.call-start
  12.5 34.7 %all-reduce.3.cloned.1.call-done = (bf16[128,1280]{1,0:T(8,128)(2,1)}, bf16[128,1280]{1,0:T(8,128)(2,1)}) async-done(((bf16[128,1280]{1,0:T(8,128)(2,1)}, bf16[128,1280]{1,0:T(8,128)(2,1)}), (bf16[128,1280]{1,0:T(8,128)(2,1)}, bf16[128,1280]{1,0:T(8,128)(2,1)})) %all-reduce.3.cloned.1.call-update) | async-done | bytes 655376 | tf_op jit(solution)/shard_map/psum | solution.py:13
  47.2 0.0 all-gather.3.cloned.1.call-update
  47.2 0.0 all-gather.5.cloned.1.call-start
  47.3 0.7 all-gather.5.cloned.1.call-update
  48.0 0.0 copy-done.1
  48.0 0.0 copy-done.5
  48.0 0.5 convolution_convert_fusion.1
  48.4 0.9 copy.12
  49.4 32.9 %all-gather.3.cloned.1.call-done = bf16[512,1280]{1,0:T(8,128)(2,1)} async-done(((bf16[128,1280]{1,0:T(8,128)(2,1)}), bf16[512,1280]{1,0:T(8,128)(2,1)}) %all-gather.3.cloned.1.call-update) | async-done | bytes 1310736 | tf_op jit(solution)/shard_map/all_gather | solution.py:83
  82.2 2.5 %constant_dynamic-update-slice_fusion.1 = bf16[1024,1280]{1,0:T(8,128)(2,1)} fusion(bf16[512,1280]{1,0:T(8,128)(2,1)} %all-gather.3.cloned.1.call-done), kind=kLoop, calls=%fused_computation.54 | loop fusion | bytes 2621440
  84.7 30.8 %all-gather.5.cloned.1.call-done = bf16[512,1280]{1,0:T(8,128)(2,1)} async-done(((bf16[128,1280]{1,0:T(8,128)(2,1)}), bf16[512,1280]{1,0:T(8,128)(2,1)}) %all-gather.5.cloned.1.call-update) | async-done | bytes 1310736 | tf_op jit(solution)/shard_map/all_gather | solution.py:84
  115.5 2.5 %constant_dynamic-update-slice_fusion = bf16[1024,1280]{1,0:T(8,128)(2,1)} fusion(bf16[1024,1280]{1,0:T(8,128)(2,1)} %constant_dynamic-update-slice_fusion.1, bf16[512,1280]{1,0:T(8,128)(2,1)} %all-gather.5.cloned.1.call-done), kind=kLoop, calls=%fused_computation.53 | loop fusion | bytes 2621440 | tf_op jit(solution)/shard_map/concatenate | solution.py:39
  118.0 3.5 %fusion.41 = (bf16[1024,640]{1,0:T(8,128)(2,1)}, bf16[1024,640]{1,0:T(8,128)(2,1)}) fusion(bf16[1024,1280]{1,0:T(8,128)(2,1)} %constant_dynamic-update-slice_fusion), kind=kLoop, calls=%fused_computation.63 | loop fusion | bytes 5242880 | tf_op jit(solution)/shard_map/slice | solution.py:40
  121.5 1.6 copy.13
  123.1 2.5 %copy.14 = bf16[1024,640]{0,1:T(8,128)(2,1)} copy(bf16[1024,640]{1,0:T(8,128)(2,1)} %get-tuple-element.8) | data formatting | bytes 2621440 | tf_op jit(solution)/shard_map/slice | solution.py:41
  125.5 2.6 %multiply_reduce_fusion = (f32[10,256]{1,0:T(8,128)S(1)}, f32[10,256,1024]{2,1,0:T(8,128)S(1)}) fusion(bf16[256,10,64]{0,2,1:T(8,128)(2,1)} %bitcast.74, bf16[1024,10,64]{0,2,1:T(8,128)(2,1)S(1)} %bitcast.69), kind=kOutput, calls=%fused_computation.2 | convolution fusion | flops 340784640 | bytes 12134400 | tf_op jit(solution)/shard_map/qhd,khd->hqk/dot_general | solution.py:42
  128.2 0.0 copy-start.3
  128.2 2.1 %fusion = f32[10,256]{1,0:T(8,128)S(1)} fusion(f32[10,256,1024]{2,1,0:T(8,128)S(1)} %get-tuple-element.26, f32[10,256]{1,0:T(8,128)S(1)} %get-tuple-element.20), kind=kLoop, calls=%fused_computation.3 | loop fusion | flops 7861760 | bytes 10506240 | tf_op jit(solution)/shard_map/reduce_sum | solution.py:48
  130.2 0.0 copy-done.3
  130.2 0.0 copy-start.6
  130.3 0.0 copy-start.7
  130.3 2.3 %fusion.19 = bf16[256,10,64]{0,2,1:T(8,128)(2,1)S(1)} fusion(bf16[1024,10,64]{0,2,1:T(8,128)(2,1)S(1)} %bitcast.77, f32[10,256,1024]{2,1,0:T(8,128)S(1)} %get-tuple-element.26, f32[10,256]{1,0:T(8,128)S(1)} %get-tuple-element.20, f32[256,10]{0,1:T(8,128)S(1)} %bitcast.82, f32[256,10]{0,1:T(8,128)S(1)} %get-tuple-element.19), kind=kOutput, calls=%fused_computation.20 | convolution fusion | flops 343900160 | bytes 12154880 | tf_op jit(solution)/shard_map/hqk,khd->qhd/dot_general | solution.py:49
  132.6 0.0 copy-start.4
  132.6 0.0 copy-done.6
  132.6 0.6 multiply_reduce_fusion.1
  133.2 0.0 copy-done.7
  133.2 0.1 multiply_convert_fusion.1
  133.4 4.3 %collective-permute-start = (bf16[1,128,640]{2,1,0:T(8,128)(2,1)S(1)}, bf16[1,128,640]{2,1,0:T(8,128)(2,1)S(1)}, u32[]{:S(2)}, u32[]{:S(2)}) collective-permute-start(bf16[1,128,640]{2,1,0:T(8,128)(2,1)S(1)} %get-tuple-element.17), channel_id=1, source_target_pairs={{0,4},{4,8},{8,12},{1,5},{5,9},{9,13},{2,6},{6,10},{10,14},{3,7},{... | collective-permute-start | bytes 491528 | tf_op jit(solution)/shard_map/ppermute | solution.py:23
  137.7 1.9 %collective-permute-start.1 = (bf16[1,128,640]{2,1,0:T(8,128)(2,1)S(1)}, bf16[1,128,640]{2,1,0:T(8,128)(2,1)S(1)}, u32[]{:S(2)}, u32[]{:S(2)}) collective-permute-start(bf16[1,128,640]{2,1,0:T(8,128)(2,1)S(1)} %get-tuple-element.18), channel_id=1, source_target_pairs={{4,0},{8,4},{12,8},{5,1},{9,5},{13,9},{6,2},{10,6},{14,10},{7,3},{... | collective-permute-start | bytes 491528 | tf_op jit(solution)/shard_map/ppermute | solution.py:24
  139.6 0.0 copy-done.4
  139.6 0.5 fusion.29
  140.1 0.0 collective-permute-done
  140.1 4.2 %collective-permute-done.1 = bf16[1,128,640]{2,1,0:T(8,128)(2,1)S(1)} collective-permute-done((bf16[1,128,640]{2,1,0:T(8,128)(2,1)S(1)}, bf16[1,128,640]{2,1,0:T(8,128)(2,1)S(1)}, u32[]{:S(2)}, u32[]{:S(2)}) %collective-permute-start.1) | collective-permute-done | bytes 163872 | tf_op jit(solution)/shard_map/ppermute | solution.py:24
  144.3 0.1 pad_maximum_fusion.3
  144.4 0.5 fusion.27
  144.9 0.0 copy-start.2
  144.9 0.5 multiply_convert_fusion
  145.4 2.1 %collective-permute-start.2 = (bf16[1,128,640]{2,1,0:T(8,128)(2,1)S(1)}, bf16[1,128,640]{2,1,0:T(8,128)(2,1)S(1)}, u32[]{:S(2)}, u32[]{:S(2)}) collective-permute-start(bf16[1,128,640]{2,1,0:T(8,128)(2,1)S(1)} %get-tuple-element.13), channel_id=1, source_target_pairs={{0,4},{4,8},{8,12},{1,5},{5,9},{9,13},{2,6},{6,10},{10,14},{3,7},{... | collective-permute-start | bytes 491528 | tf_op jit(solution)/shard_map/ppermute | solution.py:23
  147.5 2.4 %collective-permute-start.3 = (bf16[1,128,640]{2,1,0:T(8,128)(2,1)S(1)}, bf16[1,128,640]{2,1,0:T(8,128)(2,1)S(1)}, u32[]{:S(2)}, u32[]{:S(2)}) collective-permute-start(bf16[1,128,640]{2,1,0:T(8,128)(2,1)S(1)} %get-tuple-element.14), channel_id=1, source_target_pairs={{4,0},{8,4},{12,8},{5,1},{9,5},{13,9},{6,2},{10,6},{14,10},{7,3},{... | collective-permute-start | bytes 491528 | tf_op jit(solution)/shard_map/ppermute | solution.py:24
  149.9 0.0 copy-done.2
  149.9 0.5 fusion.24
  150.4 0.0 collective-permute-done.2
  150.4 3.7 %collective-permute-done.3 = bf16[1,128,640]{2,1,0:T(8,128)(2,1)S(1)} collective-permute-done((bf16[1,128,640]{2,1,0:T(8,128)(2,1)S(1)}, bf16[1,128,640]{2,1,0:T(8,128)(2,1)S(1)}, u32[]{:S(2)}, u32[]{:S(2)}) %collective-permute-start.3) | collective-permute-done | bytes 163872 | tf_op jit(solution)/shard_map/ppermute | solution.py:24
  154.1 0.1 pad_maximum_fusion.1
  154.2 0.5 fusion.22
  154.7 1.2 fusion.15
  (5 shorter events, 0.1 us)
Async XLA Ops:
  6.5 4.3 %copy-start = (bf16[640,1280]{1,0:T(8,128)(2,1)S(1)}, bf16[640,1280]{1,0:T(8,128)(2,1)}, u32[]{:S(2)}) copy-start(bf16[640,1280]{1,0:T(8,128)(2,1)} %param.11) | copy-start | bytes 4915204
  6.5 40.7 %all-reduce.3.cloned.1.call-start = ((), (), s32[]{:S(2)}) async-start(), calls=%async_computation.2 | async-start | bytes 1310720 | tf_op jit(solution)/shard_map/psum | solution.py:13
  10.8 37.2 %copy-start.1 = (bf16[2,128,640]{2,1,0:T(8,128)(2,1)S(1)}, bf16[2,128,640]{2,1,0:T(8,128)(2,1)}, u32[]{:S(2)}) copy-start(bf16[2,128,640]{2,1,0:T(8,128)(2,1)} %param.8) | copy-start | bytes 983044
  10.8 37.2 %copy-start.5 = (bf16[640,640]{1,0:T(8,128)(2,1)S(1)}, bf16[640,640]{1,0:T(8,128)(2,1)}, u32[]{:S(2)}) copy-start(bf16[640,640]{1,0:T(8,128)(2,1)} %param.10) | copy-start | bytes 2457604
  12.5 69.8 %all-gather.3.cloned.1.call-start = ((), (), s32[]{:S(2)}) async-start(), calls=%async_computation | async-start | bytes 1638400 | tf_op jit(solution)/shard_map/all_gather | solution.py:83
  47.2 68.3 %all-gather.5.cloned.1.call-start = ((), (), s32[]{:S(2)}) async-start(), calls=%async_computation.1 | async-start | bytes 1638400 | tf_op jit(solution)/shard_map/all_gather | solution.py:84
  128.2 2.1 %copy-start.3 = (bf16[1024,640]{0,1:T(8,128)(2,1)S(1)}, bf16[1024,640]{0,1:T(8,128)(2,1)}, u32[]{:S(2)}) copy-start(bf16[1024,640]{0,1:T(8,128)(2,1)} %copy.14) | copy-start | bytes 3932164
  130.2 2.3 %copy-start.6 = (bf16[640,640]{1,0:T(8,128)(2,1)S(1)}, bf16[640,640]{1,0:T(8,128)(2,1)}, u32[]{:S(2)}) copy-start(bf16[640,640]{1,0:T(8,128)(2,1)} %param.12) | copy-start | bytes 2457604
  130.3 2.9 %copy-start.7 = (f32[640]{0:T(1024)S(1)}, f32[640]{0:T(1024)}, u32[]{:S(2)}) copy-start(f32[640]{0:T(1024)} %param.13) | copy-start | bytes 7684
  132.6 7.1 %copy-start.4 = (bf16[3,640,640]{2,1,0:T(8,128)(2,1)S(1)}, bf16[3,640,640]{2,1,0:T(8,128)(2,1)}, u32[]{:S(2)}) copy-start(bf16[3,640,640]{2,1,0:T(8,128)(2,1)} %param.14) | copy-start | bytes 7372804
  133.4 6.7 %collective-permute-start = (bf16[1,128,640]{2,1,0:T(8,128)(2,1)S(1)}, bf16[1,128,640]{2,1,0:T(8,128)(2,1)S(1)}, u32[]{:S(2)}, u32[]{:S(2)}) collective-permute-start(bf16[1,128,640]{2,1,0:T(8,128)(2,1)S(1)} %get-tuple-element.17), channel_id=1, source_target_pairs={{0,4},{4,8},{8,12},{1,5},{5,9},{9,13},{2,6},{6,10},{10,14},{3,7},{... | collective-permute-start | bytes 491528 | tf_op jit(solution)/shard_map/ppermute | solution.py:23
  137.7 6.6 %collective-permute-start.1 = (bf16[1,128,640]{2,1,0:T(8,128)(2,1)S(1)}, bf16[1,128,640]{2,1,0:T(8,128)(2,1)S(1)}, u32[]{:S(2)}, u32[]{:S(2)}) collective-permute-start(bf16[1,128,640]{2,1,0:T(8,128)(2,1)S(1)} %get-tuple-element.18), channel_id=1, source_target_pairs={{4,0},{8,4},{12,8},{5,1},{9,5},{13,9},{6,2},{10,6},{14,10},{7,3},{... | collective-permute-start | bytes 491528 | tf_op jit(solution)/shard_map/ppermute | solution.py:24
  144.9 5.1 %copy-start.2 = (bf16[3,640,640]{2,1,0:T(8,128)(2,1)S(1)}, bf16[3,640,640]{2,1,0:T(8,128)(2,1)}, u32[]{:S(2)}) copy-start(bf16[3,640,640]{2,1,0:T(8,128)(2,1)} %param.15) | copy-start | bytes 7372804
  145.4 5.0 %collective-permute-start.2 = (bf16[1,128,640]{2,1,0:T(8,128)(2,1)S(1)}, bf16[1,128,640]{2,1,0:T(8,128)(2,1)S(1)}, u32[]{:S(2)}, u32[]{:S(2)}) collective-permute-start(bf16[1,128,640]{2,1,0:T(8,128)(2,1)S(1)} %get-tuple-element.13), channel_id=1, source_target_pairs={{0,4},{4,8},{8,12},{1,5},{5,9},{9,13},{2,6},{6,10},{10,14},{3,7},{... | collective-permute-start | bytes 491528 | tf_op jit(solution)/shard_map/ppermute | solution.py:23
  147.5 6.6 %collective-permute-start.3 = (bf16[1,128,640]{2,1,0:T(8,128)(2,1)S(1)}, bf16[1,128,640]{2,1,0:T(8,128)(2,1)S(1)}, u32[]{:S(2)}, u32[]{:S(2)}) collective-permute-start(bf16[1,128,640]{2,1,0:T(8,128)(2,1)S(1)} %get-tuple-element.14), channel_id=1, source_target_pairs={{4,0},{8,4},{12,8},{5,1},{9,5},{13,9},{6,2},{10,6},{14,10},{7,3},{... | collective-permute-start | bytes 491528 | tf_op jit(solution)/shard_map/ppermute | solution.py:24
Sparse Core Ops, SparseCore 0:
  12.6 34.5 all-reduce.2
  48.8 33.4 all-gather.2
  83.8 31.6 all-gather.4
where the time goes:
time: 163 us; the launch traced here: 162 us
  waiting for transfers between devices  107 us (66%)
  local copies, waits for them, and re-layouts  15.6 us (10%)
  between operations  14.7 us (9%)
  starting transfers between devices  10.8 us (7%)
  matrix products  10.2 us (6%)
  other arithmetic  4.05 us (2%)
    psum x1, waiting for transfers between devices, from_root(): return lax.psum(kept, axis)  34.7 us
    all_gather x1, waiting for transfers between devices, shards(): lax.all_gather(spread_parts[0], 'row', axis=0, tiled=True)  32.9 us
    all_gather x1, waiting for transfers between devices, shards(): lax.all_gather(spread_parts[1], 'row', axis=0, tiled=True)  30.8 us
    ppermute x2, waiting for transfers between devices, extended(): after = lax.ppermute(first, axis, down)  7.96 us
    ppermute x2, starting transfers between devices, extended(): before = lax.ppermute(last, axis, up)  6.37 us
    slice x2, local copies, waits for them, and re-layouts, absorb_keys(): key_heads = joined[:, :channels].reshape(-1, HEADS, HEAD_DIM)  5.06 us
    ppermute x2, starting transfers between devices, extended(): after = lax.ppermute(first, axis, down)  4.33 us
    dot_general x6, matrix products, temporal_mix(): jnp.dot(window, weights[offset], preferred_element_type=jnp.float32)  3.53 us
  transfers between devices with their start and end apart: 7, of which 5 were waited for; matrix products, arithmetic and copies ran while one was open for 3% of the time, Pallas kernels for 0%

commit v1 on v0

--- a/solution.py
+++ b/solution.py
@@ -6,6 +6,28 @@
 
 HEADS = 10
 HEAD_DIM = 64
+
+
+def in_order(blocks, dim):
+    shape = list(blocks.shape[1:])
+    shape[dim] *= blocks.shape[0]
+    return jnp.moveaxis(blocks, 0, dim).reshape(shape)
+
+
+def doubled(value, axis):
+    size = lax.axis_size(axis)
+    blocks = value[None]
+    for level in range(size.bit_length() - 1):
+        bit = 1 << level
+        partner_block = lax.ppermute(blocks, axis, [(i, i ^ bit) for i in range(size)])
+        both = jnp.stack([blocks, partner_block])
+        upper = lax.axis_index(axis) >> level & 1
+        blocks = jnp.where(upper == 0, both, both[::-1]).reshape(-1, *value.shape)
+    return blocks
+
+
+def collect(array, axis, dim):
+    return in_order(doubled(array, axis), dim)
 
 
 def from_root(value, axis, source):
@@ -80,7 +102,7 @@
     final = absorb(
         initial,
         (
-            lax.all_gather(spread_parts[0], "row", axis=0, tiled=True),
+            collect(spread_parts[0], "row", 0),
             lax.all_gather(spread_parts[1], "row", axis=0, tiled=True),
         ),
         jnp.int32(0),

time: 163 us -> 156 us (0.957)
  waiting for transfers between devices: 107 us -> 96.2 us
  local copies, waits for them, and re-layouts: 15.6 us -> 7.25 us
  other arithmetic: 4.05 us -> 10.4 us
  starting transfers between devices: 10.8 us -> 15.1 us
    ppermute x0 -> x2, waiting for transfers between devices: none -> 53.5 us  [doubled(): lax.ppermute(blocks, axis, [(i, i ^ bit) for i in range(size)])]
    all_gather x1 -> x0, waiting for transfers between devices: 32.9 us -> none  [shards(): lax.all_gather(spread_parts[0], 'row', axis=0, tiled=True)]
    all_gather x1, waiting for transfers between devices: 30.8 us -> 0.02 us  [shards(): lax.all_gather(spread_parts[1], 'row', axis=0, tiled=True)]
    ppermute x0 -> x2, starting transfers between devices: none -> 4.33 us  [doubled(): lax.ppermute(blocks, axis, [(i, i ^ bit) for i in range(size)])]
    slice x2 -> x1, local copies, waits for them, and re-layouts: 5.06 us -> 1.6 us  [absorb_keys(): key_heads = joined[:, :channels].reshape(-1, HEADS, HEAD_DIM)]
    another operation x0 -> x3, other arithmetic: none -> 3.2 us  [doubled(): both = jnp.stack([blocks, partner_block])]
    concatenate x0 -> x1, other arithmetic: none -> 2.97 us  [absorb_keys(): joined = jnp.concatenate(kv_pieces, axis=0)]
    unnamed x17 -> x14, local copies, waits for them, and re-layouts: 2.52 us -> 0.04 us
  transfers between devices with their start and end apart: 7 -> 8, of which waited for: 5 -> 5; matrix products, arithmetic and copies ran while one was open for 3% -> 4% of each run, Pallas kernels for 0% -> 0%
where the time goes in v1:
time: 156 us; the launch traced here: 155 us
  waiting for transfers between devices  96.2 us (62%)
  starting transfers between devices  15.1 us (10%)
  between operations  15 us (10%)
  matrix products  11.3 us (7%)
  other arithmetic  10.4 us (7%)
  local copies, waits for them, and re-layouts  7.25 us (5%)
    ppermute x2, waiting for transfers between devices, doubled(): lax.ppermute(blocks, axis, [(i, i ^ bit) for i in range(size)])  53.5 us
    psum x1, waiting for transfers between devices, from_root(): return lax.psum(kept, axis)  34.7 us
    ppermute x2, waiting for transfers between devices, extended(): after = lax.ppermute(first, axis, down)  7.96 us
    ppermute x2, starting transfers between devices, extended(): before = lax.ppermute(last, axis, up)  6.41 us
    ppermute x2, starting transfers between devices, doubled(): lax.ppermute(blocks, axis, [(i, i ^ bit) for i in range(size)])  4.33 us
    ppermute x2, starting transfers between devices, extended(): after = lax.ppermute(first, axis, down)  4.33 us
    dot_general x6, matrix products, temporal_mix(): jnp.dot(window, weights[offset], preferred_element_type=jnp.float32)  3.53 us
    another operation x3, other arithmetic, doubled(): both = jnp.stack([blocks, partner_block])  3.2 us
  transfers between devices with their start and end apart: 8, of which 5 were waited for; matrix products, arithmetic and copies ran while one was open for 4% of the time, Pallas kernels for 0%

profile of v1, /device:TPU:1, one launch (start us, length us, event | category | flops | bytes accessed | tf_op | source)
XLA Modules:
  0.0 155.3 jit_solution(17334580482452409395)
XLA Ops:
  6.5 0.0 copy-start
  6.5 0.0 all-reduce.3.cloned.1.call-start
  6.5 0.8 and_select_fusion.1
  7.3 0.6 fusion.44
  9.2 1.6 %gather_fusion = bf16[2,128,640]{2,1,0:T(8,128)(2,1)S(1)} fusion(bf16[2,128,640]{2,1,0:T(8,128)(2,1)} %param.8, s32[1024]{0:T(1024)S(1)} %pad_clamp_fusion), kind=kCustom, calls=%fused_computation | custom fusion | bytes 655368 | tf_op jit(solution)/shard_map/gather | solution.py:90
  10.8 0.0 copy-done
  10.8 0.7 convolution_convert_fusion
  11.5 0.9 slice_select_fusion.1
  12.4 0.0 copy-start.1
  12.4 0.0 all-reduce.3.cloned.1.call-update
  12.4 0.0 all-gather.2.cloned.1.call-start
  12.5 34.7 %all-reduce.3.cloned.1.call-done = (bf16[128,1280]{1,0:T(8,128)(2,1)}, bf16[128,1280]{1,0:T(8,128)(2,1)}) async-done(((bf16[128,1280]{1,0:T(8,128)(2,1)}, bf16[128,1280]{1,0:T(8,128)(2,1)}), (bf16[128,1280]{1,0:T(8,128)(2,1)}, bf16[128,1280]{1,0:T(8,128)(2,1)})) %all-reduce.3.cloned.1.call-update) | async-done | bytes 655376 | tf_op jit(solution)/shard_map/psum | solution.py:35
  47.2 1.7 %collective-permute-start = (bf16[1,128,1280]{2,1,0:T(8,128)(2,1)}, bf16[1,128,1280]{2,1,0:T(8,128)(2,1)S(1)}, u32[]{:S(2)}, u32[]{:S(2)}) collective-permute-start(bf16[1,128,1280]{2,1,0:T(8,128)(2,1)} %bitcast.90), channel_id=1, source_target_pairs={{0,1},{1,0},{2,3},{3,2},{4,5},{5,4},{6,7},{7,6},{8,9},{9,8},{10,11... | collective-permute-start | bytes 983048 | tf_op jit(solution)/shard_map/ppermute | solution.py:22
  48.8 0.0 all-gather.2.cloned.1.call-update
  48.9 6.1 %collective-permute-done = bf16[1,128,1280]{2,1,0:T(8,128)(2,1)S(1)} collective-permute-done((bf16[1,128,1280]{2,1,0:T(8,128)(2,1)}, bf16[1,128,1280]{2,1,0:T(8,128)(2,1)S(1)}, u32[]{:S(2)}, u32[]{:S(2)}) %collective-permute-start) | collective-permute-done | bytes 327712 | tf_op jit(solution)/shard_map/ppermute | solution.py:22
  55.0 1.0 pad_maximum_fusion.2
  56.0 1.0 fusion.42
  57.0 2.6 %collective-permute-start.1 = (bf16[2,128,1280]{2,1,0:T(8,128)(2,1)}, bf16[2,128,1280]{2,1,0:T(8,128)(2,1)}, u32[]{:S(2)}, u32[]{:S(2)}) collective-permute-start(bf16[2,128,1280]{2,1,0:T(8,128)(2,1)} %get-tuple-element.10), channel_id=1, source_target_pairs={{0,2},{1,3},{2,0},{3,1},{4,6},{5,7},{6,4},{7,5},{8,10},{9,11},{10,... | collective-permute-start | bytes 1966088 | tf_op jit(solution)/shard_map/ppermute | solution.py:22
  59.6 0.0 copy-done.1
  59.6 1.6 %convolution_convert_fusion.1 = bf16[256,640]{1,0:T(8,128)(2,1)S(1)} fusion(bf16[256,640]{1,0:T(8,128)(2,1)S(1)} %bitcast.82, bf16[640,640]{1,0:T(8,128)(2,1)} %param.10), kind=kOutput, calls=%fused_computation.24 | convolution fusion | flops 209879040 | bytes 1474560 | tf_op jit(solution)/shard_map/dot_general | solution.py:86
  61.2 0.9 copy.12
  62.1 47.4 %collective-permute-done.1 = bf16[2,128,1280]{2,1,0:T(8,128)(2,1)} collective-permute-done((bf16[2,128,1280]{2,1,0:T(8,128)(2,1)}, bf16[2,128,1280]{2,1,0:T(8,128)(2,1)}, u32[]{:S(2)}, u32[]{:S(2)}) %collective-permute-start.1) | collective-permute-done | bytes 655392 | tf_op jit(solution)/shard_map/ppermute | solution.py:22
  109.5 1.2 pad_maximum_fusion.1
  110.7 0.2 reverse_select_fusion
  111.0 0.0 all-gather.2.cloned.1.call-done
  111.0 3.0 %fusion.6 = (bf16[1024,640]{1,0:T(8,128)(2,1)}, bf16[1024,640]{1,0:T(8,128)(2,1)}) fusion(bf16[512,1280]{1,0:T(8,128)(2,1)S(1)} %bitcast.80, bf16[512,1280]{1,0:T(8,128)(2,1)} %all-gather.2.cloned.1.call-done), kind=kLoop, calls=%fused_computation.12 | loop fusion | flops 5242880 | bytes 5242880 | tf_op jit(solution)/shard_map/concatenate | solution.py:61
  114.0 1.6 %copy.13 = bf16[1024,640]{0,1:T(8,128)(2,1)S(1)} copy(bf16[1024,640]{1,0:T(8,128)(2,1)} %get-tuple-element.7) | data formatting | bytes 2621440 | tf_op jit(solution)/shard_map/slice | solution.py:62
  115.6 2.5 %copy.14 = bf16[1024,640]{0,1:T(8,128)(2,1)} copy(bf16[1024,640]{1,0:T(8,128)(2,1)} %get-tuple-element.8) | data formatting | bytes 2621440 | tf_op jit(solution)/shard_map/slice | solution.py:63
  118.1 2.6 %multiply_reduce_fusion = (f32[10,256]{1,0:T(8,128)S(1)}, f32[10,256,1024]{2,1,0:T(8,128)S(1)}) fusion(bf16[256,10,64]{0,2,1:T(8,128)(2,1)} %bitcast.84, bf16[1024,10,64]{0,2,1:T(8,128)(2,1)S(1)} %bitcast.78), kind=kOutput, calls=%fused_computation.2 | convolution fusion | flops 340784640 | bytes 12134400 | tf_op jit(solution)/shard_map/qhd,khd->hqk/dot_general | solution.py:64
  120.7 0.0 copy-start.3
  120.7 2.1 %fusion = f32[10,256]{1,0:T(8,128)S(1)} fusion(f32[10,256,1024]{2,1,0:T(8,128)S(1)} %get-tuple-element.28, f32[10,256]{1,0:T(8,128)S(1)} %get-tuple-element.22), kind=kLoop, calls=%fused_computation.3 | loop fusion | flops 7861760 | bytes 10506240 | tf_op jit(solution)/shard_map/reduce_sum | solution.py:70
  122.8 0.0 copy-done.3
  122.8 0.0 copy-start.5
  122.8 0.0 copy-start.6
  122.8 2.3 %fusion.20 = bf16[256,10,64]{0,2,1:T(8,128)(2,1)S(1)} fusion(bf16[1024,10,64]{0,2,1:T(8,128)(2,1)S(1)} %bitcast.87, f32[10,256,1024]{2,1,0:T(8,128)S(1)} %get-tuple-element.28, f32[10,256]{1,0:T(8,128)S(1)} %get-tuple-element.22, f32[256,10]{0,1:T(8,128)S(1)} %bitcast.95, f32[256,10]{0,1:T(8,128)S(1)} %get-tuple-element.21), kind=kOutput, calls=%fused_computation.26 | convolution fusion | flops 343900160 | bytes 12154880 | tf_op jit(solution)/shard_map/hqk,khd->qhd/dot_general | solution.py:71
  125.1 0.0 copy-start.4
  125.1 0.0 copy-done.5
  125.1 0.6 multiply_reduce_fusion.1
  125.7 0.0 copy-done.6
  125.7 0.1 multiply_convert_fusion.1
  125.9 4.4 %collective-permute-start.2 = (bf16[1,128,640]{2,1,0:T(8,128)(2,1)S(1)}, bf16[1,128,640]{2,1,0:T(8,128)(2,1)S(1)}, u32[]{:S(2)}, u32[]{:S(2)}) collective-permute-start(bf16[1,128,640]{2,1,0:T(8,128)(2,1)S(1)} %get-tuple-element.19), channel_id=1, source_target_pairs={{0,4},{4,8},{8,12},{1,5},{5,9},{9,13},{2,6},{6,10},{10,14},{3,7},{... | collective-permute-start | bytes 491528 | tf_op jit(solution)/shard_map/ppermute | solution.py:45
  130.3 1.9 %collective-permute-start.3 = (bf16[1,128,640]{2,1,0:T(8,128)(2,1)S(1)}, bf16[1,128,640]{2,1,0:T(8,128)(2,1)S(1)}, u32[]{:S(2)}, u32[]{:S(2)}) collective-permute-start(bf16[1,128,640]{2,1,0:T(8,128)(2,1)S(1)} %get-tuple-element.20), channel_id=1, source_target_pairs={{4,0},{8,4},{12,8},{5,1},{9,5},{13,9},{6,2},{10,6},{14,10},{7,3},{... | collective-permute-start | bytes 491528 | tf_op jit(solution)/shard_map/ppermute | solution.py:46
  132.2 0.0 copy-done.4
  132.2 0.5 fusion.30
  132.7 0.0 collective-permute-done.2
  132.7 4.2 %collective-permute-done.3 = bf16[1,128,640]{2,1,0:T(8,128)(2,1)S(1)} collective-permute-done((bf16[1,128,640]{2,1,0:T(8,128)(2,1)S(1)}, bf16[1,128,640]{2,1,0:T(8,128)(2,1)S(1)}, u32[]{:S(2)}, u32[]{:S(2)}) %collective-permute-start.3) | collective-permute-done | bytes 163872 | tf_op jit(solution)/shard_map/ppermute | solution.py:46
  136.9 0.1 pad_maximum_fusion.6
  137.0 0.5 fusion.28
  137.4 0.0 copy-start.2
  137.5 0.5 multiply_convert_fusion
  138.0 2.1 %collective-permute-start.4 = (bf16[1,128,640]{2,1,0:T(8,128)(2,1)S(1)}, bf16[1,128,640]{2,1,0:T(8,128)(2,1)S(1)}, u32[]{:S(2)}, u32[]{:S(2)}) collective-permute-start(bf16[1,128,640]{2,1,0:T(8,128)(2,1)S(1)} %get-tuple-element.15), channel_id=1, source_target_pairs={{0,4},{4,8},{8,12},{1,5},{5,9},{9,13},{2,6},{6,10},{10,14},{3,7},{... | collective-permute-start | bytes 491528 | tf_op jit(solution)/shard_map/ppermute | solution.py:45
  140.1 2.4 %collective-permute-start.5 = (bf16[1,128,640]{2,1,0:T(8,128)(2,1)S(1)}, bf16[1,128,640]{2,1,0:T(8,128)(2,1)S(1)}, u32[]{:S(2)}, u32[]{:S(2)}) collective-permute-start(bf16[1,128,640]{2,1,0:T(8,128)(2,1)S(1)} %get-tuple-element.16), channel_id=1, source_target_pairs={{4,0},{8,4},{12,8},{5,1},{9,5},{13,9},{6,2},{10,6},{14,10},{7,3},{... | collective-permute-start | bytes 491528 | tf_op jit(solution)/shard_map/ppermute | solution.py:46
  142.5 0.0 copy-done.2
  142.5 0.5 fusion.25
  143.0 0.0 collective-permute-done.4
  143.0 3.7 %collective-permute-done.5 = bf16[1,128,640]{2,1,0:T(8,128)(2,1)S(1)} collective-permute-done((bf16[1,128,640]{2,1,0:T(8,128)(2,1)S(1)}, bf16[1,128,640]{2,1,0:T(8,128)(2,1)S(1)}, u32[]{:S(2)}, u32[]{:S(2)}) %collective-permute-start.5) | collective-permute-done | bytes 163872 | tf_op jit(solution)/shard_map/ppermute | solution.py:46
  146.7 0.1 pad_maximum_fusion.4
  146.8 0.5 fusion.23
  147.2 1.2 fusion.16
  (5 shorter events, 0.1 us)
Async XLA Ops:
  6.5 4.3 %copy-start = (bf16[640,1280]{1,0:T(8,128)(2,1)S(1)}, bf16[640,1280]{1,0:T(8,128)(2,1)}, u32[]{:S(2)}) copy-start(bf16[640,1280]{1,0:T(8,128)(2,1)} %param.11) | copy-start | bytes 4915204
  6.5 40.6 %all-reduce.3.cloned.1.call-start = ((), (), s32[]{:S(2)}) async-start(), calls=%async_computation.1 | async-start | bytes 1310720 | tf_op jit(solution)/shard_map/psum | solution.py:35
  12.4 47.2 %copy-start.1 = (bf16[2,128,640]{2,1,0:T(8,128)(2,1)S(1)}, bf16[2,128,640]{2,1,0:T(8,128)(2,1)}, u32[]{:S(2)}) copy-start(bf16[2,128,640]{2,1,0:T(8,128)(2,1)} %param.8) | copy-start | bytes 983044
  12.4 98.6 %all-gather.2.cloned.1.call-start = ((), (), s32[]{:S(2)}) async-start(), calls=%async_computation | async-start | bytes 1638400 | tf_op jit(solution)/shard_map/all_gather | solution.py:106
  47.2 7.8 %collective-permute-start = (bf16[1,128,1280]{2,1,0:T(8,128)(2,1)}, bf16[1,128,1280]{2,1,0:T(8,128)(2,1)S(1)}, u32[]{:S(2)}, u32[]{:S(2)}) collective-permute-start(bf16[1,128,1280]{2,1,0:T(8,128)(2,1)} %bitcast.90), channel_id=1, source_target_pairs={{0,1},{1,0},{2,3},{3,2},{4,5},{5,4},{6,7},{7,6},{8,9},{9,8},{10,11... | collective-permute-start | bytes 983048 | tf_op jit(solution)/shard_map/ppermute | solution.py:22
  57.0 52.6 %collective-permute-start.1 = (bf16[2,128,1280]{2,1,0:T(8,128)(2,1)}, bf16[2,128,1280]{2,1,0:T(8,128)(2,1)}, u32[]{:S(2)}, u32[]{:S(2)}) collective-permute-start(bf16[2,128,1280]{2,1,0:T(8,128)(2,1)} %get-tuple-element.10), channel_id=1, source_target_pairs={{0,2},{1,3},{2,0},{3,1},{4,6},{5,7},{6,4},{7,5},{8,10},{9,11},{10,... | collective-permute-start | bytes 1966088 | tf_op jit(solution)/shard_map/ppermute | solution.py:22
  120.7 2.1 %copy-start.3 = (bf16[1024,640]{0,1:T(8,128)(2,1)S(1)}, bf16[1024,640]{0,1:T(8,128)(2,1)}, u32[]{:S(2)}) copy-start(bf16[1024,640]{0,1:T(8,128)(2,1)} %copy.14) | copy-start | bytes 3932164
  122.8 2.4 %copy-start.5 = (bf16[640,640]{1,0:T(8,128)(2,1)S(1)}, bf16[640,640]{1,0:T(8,128)(2,1)}, u32[]{:S(2)}) copy-start(bf16[640,640]{1,0:T(8,128)(2,1)} %param.12) | copy-start | bytes 2457604
  122.8 2.9 %copy-start.6 = (f32[640]{0:T(1024)S(1)}, f32[640]{0:T(1024)}, u32[]{:S(2)}) copy-start(f32[640]{0:T(1024)} %param.13) | copy-start | bytes 7684
  125.1 7.1 %copy-start.4 = (bf16[3,640,640]{2,1,0:T(8,128)(2,1)S(1)}, bf16[3,640,640]{2,1,0:T(8,128)(2,1)}, u32[]{:S(2)}) copy-start(bf16[3,640,640]{2,1,0:T(8,128)(2,1)} %param.14) | copy-start | bytes 7372804
  125.9 6.8 %collective-permute-start.2 = (bf16[1,128,640]{2,1,0:T(8,128)(2,1)S(1)}, bf16[1,128,640]{2,1,0:T(8,128)(2,1)S(1)}, u32[]{:S(2)}, u32[]{:S(2)}) collective-permute-start(bf16[1,128,640]{2,1,0:T(8,128)(2,1)S(1)} %get-tuple-element.19), channel_id=1, source_target_pairs={{0,4},{4,8},{8,12},{1,5},{5,9},{9,13},{2,6},{6,10},{10,14},{3,7},{... | collective-permute-start | bytes 491528 | tf_op jit(solution)/shard_map/ppermute | solution.py:45
  130.3 6.6 %collective-permute-start.3 = (bf16[1,128,640]{2,1,0:T(8,128)(2,1)S(1)}, bf16[1,128,640]{2,1,0:T(8,128)(2,1)S(1)}, u32[]{:S(2)}, u32[]{:S(2)}) collective-permute-start(bf16[1,128,640]{2,1,0:T(8,128)(2,1)S(1)} %get-tuple-element.20), channel_id=1, source_target_pairs={{4,0},{8,4},{12,8},{5,1},{9,5},{13,9},{6,2},{10,6},{14,10},{7,3},{... | collective-permute-start | bytes 491528 | tf_op jit(solution)/shard_map/ppermute | solution.py:46
  137.4 5.1 %copy-start.2 = (bf16[3,640,640]{2,1,0:T(8,128)(2,1)S(1)}, bf16[3,640,640]{2,1,0:T(8,128)(2,1)}, u32[]{:S(2)}) copy-start(bf16[3,640,640]{2,1,0:T(8,128)(2,1)} %param.15) | copy-start | bytes 7372804
  138.0 5.0 %collective-permute-start.4 = (bf16[1,128,640]{2,1,0:T(8,128)(2,1)S(1)}, bf16[1,128,640]{2,1,0:T(8,128)(2,1)S(1)}, u32[]{:S(2)}, u32[]{:S(2)}) collective-permute-start(bf16[1,128,640]{2,1,0:T(8,128)(2,1)S(1)} %get-tuple-element.15), channel_id=1, source_target_pairs={{0,4},{4,8},{8,12},{1,5},{5,9},{9,13},{2,6},{6,10},{10,14},{3,7},{... | collective-permute-start | bytes 491528 | tf_op jit(solution)/shard_map/ppermute | solution.py:45
  140.1 6.6 %collective-permute-start.5 = (bf16[1,128,640]{2,1,0:T(8,128)(2,1)S(1)}, bf16[1,128,640]{2,1,0:T(8,128)(2,1)S(1)}, u32[]{:S(2)}, u32[]{:S(2)}) collective-permute-start(bf16[1,128,640]{2,1,0:T(8,128)(2,1)S(1)} %get-tuple-element.16), channel_id=1, source_target_pairs={{4,0},{8,4},{12,8},{5,1},{9,5},{13,9},{6,2},{10,6},{14,10},{7,3},{... | collective-permute-start | bytes 491528 | tf_op jit(solution)/shard_map/ppermute | solution.py:46
Sparse Core Ops, SparseCore 0:
  12.6 34.5 all-reduce.2
  49.0 58.5 all-gather.1
